TPU v7x, 32 devices: a whole 2x2x4 slice. The times are simulated.
32 devices in a mesh: groups: 2 (over x), wide: 16 (over z, y, core).
Axes of the slice: x: 2, y: 2, z: 4, core: 2. Of those that a mesh axis runs over, the one named last changes fastest.
Arguments:
- retarded_tiles: bfloat16 [32, 16, 2, 128, 128], P(('groups', 'wide')), parts along dimension 0, may hold values from -0.0625 to 0.0625
- tile_lags: int32 [32, 16, 2], P(('groups', 'wide')), parts along dimension 0, may hold values from 1 to 4, as said below
- block_owner: int32 [32], P('groups'), parts along dimension 0, may hold values from 0 to 15, each once
- later_current: bfloat16 [4, 4096, 128], P(None, ('groups', 'wide')), parts along dimension 1, may hold values from -6 to 6
- excitation: float32 [3, 4096, 128], P(None, ('groups', 'wide')), parts along dimension 1, may hold values from -6 to 6
- inverse_blocks: float32 [32, 128, 128], P(('groups', 'wide')), parts along dimension 0, may hold values from -0.5 to 0.5
Outputs:
- adjoint_current: float32 [3, 4096, 128], P(None, ('groups', 'wide')), parts along dimension 1
There are 2 independent parts, one for each index of `groups`. A program takes and returns all parts, laid end to end along the dimension named above; each array names one. Nothing has to cross between parts.
Inputs may be any that keep to these rules, and one draw needn't show every extreme that they name: `tile_lags`: the two slots of every tile name different lags. `block_owner`: each edge block is named once.
All inputs are finite; a program needn't handle non-finite values.
Results may differ from a plain program's by a relative error of at most 0.003.
Values may be sent and summed in bfloat16 or wider, within the bound.
No kernel may reach another device: no remote copies, remote signals or barrier semaphores. Data moves between devices by JAX's collectives and lax.ppermute only.
A program may use at most 128 MiB of HBM per device.

v0:
```python
import jax
import jax.numpy as jnp
from jax import lax
from jax.sharding import PartitionSpec as P


def per_device(retarded_tiles, tile_lags, block_owner, later_current, excitation, inverse_blocks):
    tile_size = retarded_tiles.shape[-1]
    pulses = later_current.shape[-1]
    lag_count = later_current.shape[0]
    step_count = excitation.shape[0]
    column_order = jnp.argsort(block_owner)
    local_tiles = jnp.take(retarded_tiles[0], column_order, axis=0)
    local_lags = jnp.take(tile_lags[0], column_order, axis=0)
    inverse = inverse_blocks[0]
    results = [None] * step_count
    later = lax.all_gather(later_current, "wide", axis=1, tiled=True)
    history = {}
    for offset in range(lag_count):
        history[step_count + offset] = later[offset].reshape(-1, tile_size, pulses)
    for moment in range(step_count - 1, -1, -1):
        chosen = jnp.zeros(local_lags.shape + (tile_size, pulses), jnp.bfloat16)
        for delay in range(1, lag_count + 1):
            chosen = jnp.where(
                (local_lags == delay)[:, :, None, None], history[moment + delay][:, None], chosen
            )
        retarded = jnp.einsum(
            "jspq,jspr->qr", local_tiles, chosen, preferred_element_type=jnp.float32
        )
        source = excitation[moment] - retarded
        current = jnp.dot(
            inverse.T, source, precision=lax.Precision.HIGHEST, preferred_element_type=jnp.float32
        )
        results[moment] = current
        if moment > 0:
            rounded = current.astype(jnp.bfloat16)[None]
            history[moment] = lax.all_gather(rounded, "wide", axis=0, tiled=True)
    return jnp.stack(results)


def solution(mesh):
    in_specs = (
        P(("groups", "wide"), None, None, None, None),
        P(("groups", "wide"), None, None),
        P("groups"),
        P(None, ("groups", "wide"), None),
        P(None, ("groups", "wide"), None),
        P(("groups", "wide"), None, None),
    )
    out_specs = P(None, ("groups", "wide"), None)
    return jax.shard_map(
        per_device, mesh=mesh, in_specs=in_specs, out_specs=out_specs, check_vma=False
    )
```

profile of v0, /device:TPU:0, one launch (start us, length us, event | category | flops | bytes accessed | tf_op | source)
XLA Modules:
  0.0 111.3 jit_solution(3623664762194302780)
XLA Ops:
  6.5 0.0 copy-start
  6.5 0.0 all-gather.4.cloned.1.call-start
  6.5 0.7 all-gather.4.cloned.1.call-update
  7.3 0.8 copy.7
  8.0 1.9 %sort.17 = (s32[16]{0:T(128)}, s32[16]{0:T(128)S(1)}) sort(s32[16]{0:T(128)} %param.8, s32[16]{0:T(128)S(1)} %iota.4), dimensions={0}, to_apply=%region_0.0 | sort | flops 64 | bytes 256 | tf_op jit(solution)/shard_map/jit(argsort)/sort | solution.py:12
  9.9 0.6 gather_fusion.1
  10.5 0.0 copy-done
  10.5 0.7 gather_fusion
  11.3 0.1 select_compare_fusion.3
  11.4 42.4 %all-gather.4.cloned.1.call-done = bf16[4,2048,128]{2,1,0:T(8,128)(2,1)} async-done(((bf16[4,128,128]{2,1,0:T(8,128)(2,1)}), bf16[4,2048,128]{2,1,0:T(8,128)(2,1)}) %all-gather.4.cloned.1.call-update) | async-done | bytes 2097168 | tf_op jit(solution)/shard_map/all_gather | solution.py:17
  53.7 1.7 %fusion.50 = (bf16[1,2048,128]{2,1,0:T(8,128)(2,1)S(1)}, bf16[1,2048,128]{2,1,0:T(8,128)(2,1)S(1)}, bf16[1,2048,128]{2,1,0:T(8,128)(2,1)S(1)}, bf16[1,2048,128]{2,1,0:T(8,128)(2,1)S(1)}) fusion(bf16[4,2048,128]{2,1,0:T(8,128)(2,1)} %all-gather.4.cloned.1.call-done), kind=kLoop, calls=%fused_computation.67 | loop fusion | bytes 4194304 | tf_op jit(solution)/shard_map/slice | solution.py:20
  55.4 0.0 copy-start.2
  55.4 0.0 copy-start.3
  55.4 0.0 copy-start.4
  55.4 0.0 copy-start.1
  55.4 1.9 %fusion = f32[128,128]{1,0:T(8,128)S(1)} fusion(pred[16,2]{1,0:T(8,128)(4,1)S(1)} %get-tuple-element.14, pred[16,2]{1,0:T(8,128)(4,1)S(1)} %get-tuple-element.13, pred[16,2]{1,0:T(8,128)(4,1)S(1)} %get-tuple-element.12, pred[16,2]{1,0:T(8,128)(4,1)S(1)} %get-tuple-element.11, bf16[16,128,128]{2,1,0:T(8,128)(2,1)S(1)} %bitcast.68, ...), kind=kOutput, calls=%fused_computation.6 | convolution fusion | flops 136855552 | bytes 3276944 | tf_op jit(solution)/shard_map/jspq,jspr->qr/dot_general | solution.py:27
  57.3 0.0 copy-done.2
  57.3 0.0 copy-done.3
  57.4 0.0 copy-done.4
  57.4 0.0 copy-done.1
  57.4 0.3 bitcast_convert_fusion.1
  57.7 20.6 %all-gather = bf16[2048,128]{0,1:T(8,128)(2,1)S(1)} all-gather(bf16[128,128]{0,1:T(8,128)(2,1)S(1)} %get-tuple-element.15), channel_id=2, replica_groups=mesh['groups'=2,'wide'=16] {'wide'}, dimensions={0}, use_global_device_ids=true | all-gather | bytes 557056 | tf_op jit(solution)/shard_map/all_gather | solution.py:37
  78.3 0.3 copy.14
  78.6 2.3 %fusion.1 = f32[128,128]{1,0:T(8,128)S(1)} fusion(pred[16,2]{1,0:T(8,128)(4,1)S(1)} %get-tuple-element.14, pred[16,2]{1,0:T(8,128)(4,1)S(1)} %get-tuple-element.13, pred[16,2]{1,0:T(8,128)(4,1)S(1)} %get-tuple-element.12, pred[16,2]{1,0:T(8,128)(4,1)S(1)} %get-tuple-element.11, bf16[16,128,128]{2,1,0:T(8,128)(2,1)S(1)} %bitcast.59, ...), kind=kOutput, calls=%fused_computation.7 | convolution fusion | flops 136855552 | bytes 3276944 | tf_op jit(solution)/shard_map/jspq,jspr->qr/dot_general | solution.py:27
  80.8 0.3 bitcast_convert_fusion
  81.1 18.9 %all-gather.1 = bf16[2048,128]{0,1:T(8,128)(2,1)S(1)} all-gather(bf16[128,128]{0,1:T(8,128)(2,1)S(1)} %get-tuple-element.17), channel_id=3, replica_groups=mesh['groups'=2,'wide'=16] {'wide'}, dimensions={0}, use_global_device_ids=true | all-gather | bytes 557056 | tf_op jit(solution)/shard_map/all_gather | solution.py:37
  100.0 1.0 copy.15
  101.0 2.3 %fusion.2 = f32[128,128]{1,0:T(8,128)S(1)} fusion(pred[16,2]{1,0:T(8,128)(4,1)S(1)} %get-tuple-element.14, pred[16,2]{1,0:T(8,128)(4,1)S(1)} %get-tuple-element.13, pred[16,2]{1,0:T(8,128)(4,1)S(1)} %get-tuple-element.12, pred[16,2]{1,0:T(8,128)(4,1)S(1)} %get-tuple-element.11, bf16[16,128,128]{2,1,0:T(8,128)(2,1)} %bitcast.61, ...), kind=kOutput, calls=%fused_computation.8 | convolution fusion | flops 136855552 | bytes 3276944 | tf_op jit(solution)/shard_map/jspq,jspr->qr/dot_general | solution.py:27
  103.3 0.3 convolution_bitcast_fusion
  103.6 0.8 copy.10
  (5 shorter events, 0.0 us)
Async XLA Ops:
  6.5 4.0 %copy-start = (bf16[1,16,2,128,128]{4,3,2,1,0:T(8,128)(2,1)S(1)}, bf16[1,16,2,128,128]{4,3,2,1,0:T(8,128)(2,1)}, u32[]{:S(2)}) copy-start(bf16[1,16,2,128,128]{4,3,2,1,0:T(8,128)(2,1)} %param.6) | copy-start | bytes 3145732
  6.5 47.2 %all-gather.4.cloned.1.call-start = ((), (), s32[]{:S(2)}) async-start(), calls=%async_computation | async-start | bytes 2228224 | tf_op jit(solution)/shard_map/all_gather | solution.py:17
  55.4 2.0 %copy-start.2 = (bf16[1,2048,128]{2,1,0:T(8,128)(2,1)}, bf16[1,2048,128]{2,1,0:T(8,128)(2,1)S(1)}, u32[]{:S(2)}) copy-start(bf16[1,2048,128]{2,1,0:T(8,128)(2,1)S(1)} %get-tuple-element.7) | copy-start | bytes 1572868
  55.4 2.0 %copy-start.3 = (bf16[1,2048,128]{2,1,0:T(8,128)(2,1)}, bf16[1,2048,128]{2,1,0:T(8,128)(2,1)S(1)}, u32[]{:S(2)}) copy-start(bf16[1,2048,128]{2,1,0:T(8,128)(2,1)S(1)} %get-tuple-element.10) | copy-start | bytes 1572868
  55.4 2.0 %copy-start.4 = (bf16[1,2048,128]{2,1,0:T(8,128)(2,1)}, bf16[1,2048,128]{2,1,0:T(8,128)(2,1)S(1)}, u32[]{:S(2)}) copy-start(bf16[1,2048,128]{2,1,0:T(8,128)(2,1)S(1)} %get-tuple-element.8) | copy-start | bytes 1572868
  55.4 2.0 %copy-start.1 = (f32[1,128,128]{2,1,0:T(8,128)S(1)}, f32[1,128,128]{2,1,0:T(8,128)}, u32[]{:S(2)}) copy-start(f32[1,128,128]{2,1,0:T(8,128)} %param.11) | copy-start | bytes 196612
Sparse Core Ops, SparseCore 0:
  9.5 44.1 all-gather.3
where the time goes:
time: 112 us; the launch traced here: 111 us
  waiting for transfers between devices  43.1 us (38%)
  blocking collectives  39.5 us (35%)
  between operations  13.5 us (12%)
  matrix products  7.31 us (7%)
  local copies, waits for them, and re-layouts  5.84 us (5%)
  other arithmetic  2.01 us (2%)
    all_gather x1, waiting for transfers between devices, per_device(): later = lax.all_gather(later_current, 'wide', axis=1, tiled=True)  42.4 us
    all_gather x2, blocking collectives, per_device(): history[moment] = lax.all_gather(rounded, 'wide', axis=0, tiled=True)  39.5 us
    dot_general x3, matrix products, per_device(): jnp.einsum('jspq,jspr->qr', local_tiles, chosen, preferred_element_type=j...  6.46 us
  transfers between devices with their start and end apart: 1, of which 1 were waited for; matrix products, arithmetic and copies ran while one was open for 4% of the time, Pallas kernels for 0%

commit v1 on v0

--- a/solution.py
+++ b/solution.py
@@ -2,6 +2,22 @@
 import jax.numpy as jnp
 from jax import lax
 from jax.sharding import PartitionSpec as P
+
+
+def ring_gather(x, axis, dim):
+    ways, here, turn = (lax.axis_size(axis), lax.axis_index(axis), x.shape[dim])
+    dims = [n * ways if d == dim else n for d, n in enumerate(x.shape)]
+    full = lax.dynamic_update_slice_in_dim(jnp.zeros(dims, x.dtype), x, here * turn, axis=dim)
+    going_up = going_down = x
+    for far in range(1, ways // 2 + 1):
+        going_up = lax.ppermute(going_up, axis, [(d, (d + 1) % ways) for d in range(ways)])
+        full = lax.dynamic_update_slice_in_dim(full, going_up, (here - far) % ways * turn, axis=dim)
+        if 2 * far < ways:
+            going_down = lax.ppermute(going_down, axis, [(d, (d - 1) % ways) for d in range(ways)])
+            full = lax.dynamic_update_slice_in_dim(
+                full, going_down, (here + far) % ways * turn, axis=dim
+            )
+    return full
 
 
 def per_device(retarded_tiles, tile_lags, block_owner, later_current, excitation, inverse_blocks):
@@ -34,7 +50,7 @@
         results[moment] = current
         if moment > 0:
             rounded = current.astype(jnp.bfloat16)[None]
-            history[moment] = lax.all_gather(rounded, "wide", axis=0, tiled=True)
+            history[moment] = ring_gather(rounded, "wide", 0)
     return jnp.stack(results)
 
 

time: 112 us -> 170 us (1.52)
  starting transfers between devices: 0.01 us -> 63.5 us
  blocking collectives: 39.5 us -> 0 us
  waiting for transfers between devices: 43.1 us -> 74.3 us
  local copies, waits for them, and re-layouts: 5.84 us -> 8.73 us
    ppermute x0 -> x30, starting transfers between devices: none -> 63.5 us  [the longest x14 62.3 us: ring_gather(): lax.ppermute(going_down, axis, [(d, (d - 1) % ways) for d in range(ways)])]
    all_gather x2 -> x0, blocking collectives: 39.5 us -> none  [per_device(): history[moment] = lax.all_gather(rounded, 'wide', axis=0, tiled=True)]
    ppermute x0 -> x30, waiting for transfers between devices: none -> 31.6 us  [the longest x16 31.5 us: ring_gather(): lax.ppermute(going_up, axis, [(d, (d + 1) % ways) for d in range(ways)])]
    ppermute x0 -> x30, local copies, waits for them, and re-layouts: none -> 3.3 us  [the longest x16 1.75 us: ring_gather(): lax.ppermute(going_up, axis, [(d, (d + 1) % ways) for d in range(ways)])]
  transfers between devices with their start and end apart: 1 -> 31, of which waited for: 1 -> 17; matrix products, arithmetic and copies ran while one was open for 4% -> 5% of each run, Pallas kernels for 0% -> 0%
where the time goes in v1:
time: 170 us
  waiting for transfers between devices  74.3 us (44%)
  starting transfers between devices  63.5 us (37%)
  between operations  14.4 us (8%)
  local copies, waits for them, and re-layouts  8.73 us (5%)
  matrix products  7.02 us (4%)
  other arithmetic  2.02 us (1%)
    ppermute x14, starting transfers between devices, ring_gather(): lax.ppermute(going_down, axis, [(d, (d - 1) % ways) for d in range(ways)])  62.3 us
    all_gather x1, waiting for transfers between devices, per_device(): later = lax.all_gather(later_current, 'wide', axis=1, tiled=True)  42 us
    ppermute x16, waiting for transfers between devices, ring_gather(): lax.ppermute(going_up, axis, [(d, (d + 1) % ways) for d in range(ways)])  31.5 us
    dot_general x3, matrix products, per_device(): jnp.einsum('jspq,jspr->qr', local_tiles, chosen, preferred_element_type=j...  6.16 us
  transfers between devices with their start and end apart: 31, of which 17 were waited for; matrix products, arithmetic and copies ran while one was open for 5% of the time, Pallas kernels for 0%

profile of v1, /device:TPU:0, one launch (start us, length us, event | category | flops | bytes accessed | tf_op | source)
XLA Modules:
  0.0 170.0 jit_solution(2720414576977639138)
XLA Ops:
  8.3 1.9 %sort.17 = (s32[16]{0:T(128)}, s32[16]{0:T(128)S(1)}) sort(s32[16]{0:T(128)} %param.8, s32[16]{0:T(128)S(1)} %iota.4), dimensions={0}, to_apply=%region_0.0 | sort | flops 64 | bytes 256 | tf_op jit(solution)/shard_map/jit(argsort)/sort | solution.py:28
  11.7 42.0 %all-gather.2.cloned.1.call-done = bf16[4,2048,128]{2,1,0:T(8,128)(2,1)} async-done(((bf16[4,128,128]{2,1,0:T(8,128)(2,1)}), bf16[4,2048,128]{2,1,0:T(8,128)(2,1)}) %all-gather.2.cloned.1.call-update) | async-done | bytes 2097168 | tf_op jit(solution)/shard_map/all_gather | solution.py:33
  53.7 1.7 fusion.52
  55.4 1.9 %fusion = f32[128,128]{1,0:T(8,128)S(1)} fusion(pred[16,2]{1,0:T(8,128)(4,1)S(1)} %get-tuple-element.14, pred[16,2]{1,0:T(8,128)(4,1)S(1)} %get-tuple-element.13, pred[16,2]{1,0:T(8,128)(4,1)S(1)} %get-tuple-element.12, pred[16,2]{1,0:T(8,128)(4,1)S(1)} %get-tuple-element.11, bf16[16,128,128]{2,1,0:T(8,128)(2,1)S(1)} %bitcast.69, ...), kind=kOutput, calls=%fused_computation.6 | convolution fusion | flops 136855552 | bytes 3276944 | tf_op jit(solution)/shard_map/jspq,jspr->qr/dot_general | solution.py:43
  58.1 4.2 %collective-permute-start.1 = (bf16[1,128,128]{1,2,0:T(8,128)(2,1)S(1)}, bf16[1,128,128]{1,2,0:T(8,128)(2,1)S(1)}, u32[]{:S(2)}, u32[]{:S(2)}) collective-permute-start(bf16[1,128,128]{1,2,0:T(8,128)(2,1)S(1)} %fusion.47), channel_id=1, source_target_pairs={{0,15},{1,0},{2,1},{3,2},{4,3},{5,4},{6,5},{7,6},{8,7},{9,8},{10,9... | collective-permute-start | bytes 98312 | tf_op jit(solution)/shard_map/ppermute | solution.py:16
  62.4 1.5 collective-permute-done
  64.2 4.5 %collective-permute-start.3 = (bf16[1,128,128]{1,2,0:T(8,128)(2,1)S(1)}, bf16[1,128,128]{1,2,0:T(8,128)(2,1)S(1)}, u32[]{:S(2)}, u32[]{:S(2)}) collective-permute-start(bf16[1,128,128]{1,2,0:T(8,128)(2,1)S(1)} %collective-permute-done.1), channel_id=1, source_target_pairs={{0,15},{1,0},{2,1},{3,2},{4,3},{5,4},{6,5},{7,6},{8,7},{9,8},{10,9... | collective-permute-start | bytes 98312 | tf_op jit(solution)/shard_map/ppermute | solution.py:16
  68.7 1.4 collective-permute-done.2
  70.4 4.5 %collective-permute-start.5 = (bf16[1,128,128]{1,2,0:T(8,128)(2,1)S(1)}, bf16[1,128,128]{1,2,0:T(8,128)(2,1)S(1)}, u32[]{:S(2)}, u32[]{:S(2)}) collective-permute-start(bf16[1,128,128]{1,2,0:T(8,128)(2,1)S(1)} %collective-permute-done.3), channel_id=1, source_target_pairs={{0,15},{1,0},{2,1},{3,2},{4,3},{5,4},{6,5},{7,6},{8,7},{9,8},{10,9... | collective-permute-start | bytes 98312 | tf_op jit(solution)/shard_map/ppermute | solution.py:16
  74.9 1.4 collective-permute-done.4
  76.7 4.5 %collective-permute-start.7 = (bf16[1,128,128]{1,2,0:T(8,128)(2,1)S(1)}, bf16[1,128,128]{1,2,0:T(8,128)(2,1)S(1)}, u32[]{:S(2)}, u32[]{:S(2)}) collective-permute-start(bf16[1,128,128]{1,2,0:T(8,128)(2,1)S(1)} %collective-permute-done.5), channel_id=1, source_target_pairs={{0,15},{1,0},{2,1},{3,2},{4,3},{5,4},{6,5},{7,6},{8,7},{9,8},{10,9... | collective-permute-start | bytes 98312 | tf_op jit(solution)/shard_map/ppermute | solution.py:16
  81.1 1.4 collective-permute-done.6
  82.9 4.5 %collective-permute-start.9 = (bf16[1,128,128]{1,2,0:T(8,128)(2,1)S(1)}, bf16[1,128,128]{1,2,0:T(8,128)(2,1)S(1)}, u32[]{:S(2)}, u32[]{:S(2)}) collective-permute-start(bf16[1,128,128]{1,2,0:T(8,128)(2,1)S(1)} %collective-permute-done.7), channel_id=1, source_target_pairs={{0,15},{1,0},{2,1},{3,2},{4,3},{5,4},{6,5},{7,6},{8,7},{9,8},{10,9... | collective-permute-start | bytes 98312 | tf_op jit(solution)/shard_map/ppermute | solution.py:16
  87.4 1.4 collective-permute-done.8
  89.1 4.5 %collective-permute-start.11 = (bf16[1,128,128]{1,2,0:T(8,128)(2,1)S(1)}, bf16[1,128,128]{1,2,0:T(8,128)(2,1)S(1)}, u32[]{:S(2)}, u32[]{:S(2)}) collective-permute-start(bf16[1,128,128]{1,2,0:T(8,128)(2,1)S(1)} %collective-permute-done.9), channel_id=1, source_target_pairs={{0,15},{1,0},{2,1},{3,2},{4,3},{5,4},{6,5},{7,6},{8,7},{9,8},{10,9... | collective-permute-start | bytes 98312 | tf_op jit(solution)/shard_map/ppermute | solution.py:16
  95.3 4.5 %collective-permute-start.13 = (bf16[1,128,128]{1,2,0:T(8,128)(2,1)S(1)}, bf16[1,128,128]{1,2,0:T(8,128)(2,1)S(1)}, u32[]{:S(2)}, u32[]{:S(2)}) collective-permute-start(bf16[1,128,128]{1,2,0:T(8,128)(2,1)S(1)} %collective-permute-done.11), channel_id=1, source_target_pairs={{0,15},{1,0},{2,1},{3,2},{4,3},{5,4},{6,5},{7,6},{8,7},{9,8},{10,9... | collective-permute-start | bytes 98312 | tf_op jit(solution)/shard_map/ppermute | solution.py:16
  101.6 5.9 %collective-permute-done.14 = bf16[1,128,128]{1,2,0:T(8,128)(2,1)S(1)} collective-permute-done((bf16[1,128,128]{1,2,0:T(8,128)(2,1)S(1)}, bf16[1,128,128]{1,2,0:T(8,128)(2,1)S(1)}, u32[]{:S(2)}, u32[]{:S(2)}) %collective-permute-start.14) | collective-permute-done | bytes 32800 | tf_op jit(solution)/shard_map/ppermute | solution.py:13
  107.6 2.1 %fusion.1 = f32[128,128]{1,0:T(8,128)S(1)} fusion(pred[16,2]{1,0:T(8,128)(4,1)S(1)} %get-tuple-element.14, pred[16,2]{1,0:T(8,128)(4,1)S(1)} %get-tuple-element.13, pred[16,2]{1,0:T(8,128)(4,1)S(1)} %get-tuple-element.12, pred[16,2]{1,0:T(8,128)(4,1)S(1)} %get-tuple-element.11, bf16[16,128,128]{2,1,0:T(8,128)(2,1)S(1)} %constant_dynamic-update-slice_fusion.16, ...), kind=kOutput, calls=%fused_computation.7 | convolution fusion | flops 136855552 | bytes 3276944 | tf_op jit(solution)/shard_map/jspq,jspr->qr/dot_general | solution.py:43
  110.2 4.4 %collective-permute-start.16 = (bf16[1,128,128]{1,2,0:T(8,128)(2,1)S(1)}, bf16[1,128,128]{1,2,0:T(8,128)(2,1)S(1)}, u32[]{:S(2)}, u32[]{:S(2)}) collective-permute-start(bf16[1,128,128]{1,2,0:T(8,128)(2,1)S(1)} %fusion.48), channel_id=1, source_target_pairs={{0,15},{1,0},{2,1},{3,2},{4,3},{5,4},{6,5},{7,6},{8,7},{9,8},{10,9... | collective-permute-start | bytes 98312 | tf_op jit(solution)/shard_map/ppermute | solution.py:16
  114.8 1.5 collective-permute-done.15
  116.6 4.5 %collective-permute-start.18 = (bf16[1,128,128]{1,2,0:T(8,128)(2,1)S(1)}, bf16[1,128,128]{1,2,0:T(8,128)(2,1)S(1)}, u32[]{:S(2)}, u32[]{:S(2)}) collective-permute-start(bf16[1,128,128]{1,2,0:T(8,128)(2,1)S(1)} %collective-permute-done.16), channel_id=1, source_target_pairs={{0,15},{1,0},{2,1},{3,2},{4,3},{5,4},{6,5},{7,6},{8,7},{9,8},{10,9... | collective-permute-start | bytes 98312 | tf_op jit(solution)/shard_map/ppermute | solution.py:16
  121.0 1.4 collective-permute-done.17
  122.8 4.5 %collective-permute-start.20 = (bf16[1,128,128]{1,2,0:T(8,128)(2,1)S(1)}, bf16[1,128,128]{1,2,0:T(8,128)(2,1)S(1)}, u32[]{:S(2)}, u32[]{:S(2)}) collective-permute-start(bf16[1,128,128]{1,2,0:T(8,128)(2,1)S(1)} %collective-permute-done.18), channel_id=1, source_target_pairs={{0,15},{1,0},{2,1},{3,2},{4,3},{5,4},{6,5},{7,6},{8,7},{9,8},{10,9... | collective-permute-start | bytes 98312 | tf_op jit(solution)/shard_map/ppermute | solution.py:16
  127.3 1.4 collective-permute-done.19
  129.0 4.5 %collective-permute-start.22 = (bf16[1,128,128]{1,2,0:T(8,128)(2,1)S(1)}, bf16[1,128,128]{1,2,0:T(8,128)(2,1)S(1)}, u32[]{:S(2)}, u32[]{:S(2)}) collective-permute-start(bf16[1,128,128]{1,2,0:T(8,128)(2,1)S(1)} %collective-permute-done.20), channel_id=1, source_target_pairs={{0,15},{1,0},{2,1},{3,2},{4,3},{5,4},{6,5},{7,6},{8,7},{9,8},{10,9... | collective-permute-start | bytes 98312 | tf_op jit(solution)/shard_map/ppermute | solution.py:16
  133.5 1.4 collective-permute-done.21
  135.2 4.5 %collective-permute-start.24 = (bf16[1,128,128]{1,2,0:T(8,128)(2,1)S(1)}, bf16[1,128,128]{1,2,0:T(8,128)(2,1)S(1)}, u32[]{:S(2)}, u32[]{:S(2)}) collective-permute-start(bf16[1,128,128]{1,2,0:T(8,128)(2,1)S(1)} %collective-permute-done.22), channel_id=1, source_target_pairs={{0,15},{1,0},{2,1},{3,2},{4,3},{5,4},{6,5},{7,6},{8,7},{9,8},{10,9... | collective-permute-start | bytes 98312 | tf_op jit(solution)/shard_map/ppermute | solution.py:16
  139.7 1.4 collective-permute-done.23
  141.5 4.5 %collective-permute-start.26 = (bf16[1,128,128]{1,2,0:T(8,128)(2,1)S(1)}, bf16[1,128,128]{1,2,0:T(8,128)(2,1)S(1)}, u32[]{:S(2)}, u32[]{:S(2)}) collective-permute-start(bf16[1,128,128]{1,2,0:T(8,128)(2,1)S(1)} %collective-permute-done.24), channel_id=1, source_target_pairs={{0,15},{1,0},{2,1},{3,2},{4,3},{5,4},{6,5},{7,6},{8,7},{9,8},{10,9... | collective-permute-start | bytes 98312 | tf_op jit(solution)/shard_map/ppermute | solution.py:16
  147.7 4.5 %collective-permute-start.28 = (bf16[1,128,128]{1,2,0:T(8,128)(2,1)S(1)}, bf16[1,128,128]{1,2,0:T(8,128)(2,1)S(1)}, u32[]{:S(2)}, u32[]{:S(2)}) collective-permute-start(bf16[1,128,128]{1,2,0:T(8,128)(2,1)S(1)} %collective-permute-done.26), channel_id=1, source_target_pairs={{0,15},{1,0},{2,1},{3,2},{4,3},{5,4},{6,5},{7,6},{8,7},{9,8},{10,9... | collective-permute-start | bytes 98312 | tf_op jit(solution)/shard_map/ppermute | solution.py:16
  153.9 5.9 %collective-permute-done.29 = bf16[1,128,128]{1,2,0:T(8,128)(2,1)S(1)} collective-permute-done((bf16[1,128,128]{1,2,0:T(8,128)(2,1)S(1)}, bf16[1,128,128]{1,2,0:T(8,128)(2,1)S(1)}, u32[]{:S(2)}, u32[]{:S(2)}) %collective-permute-start.29) | collective-permute-done | bytes 32800 | tf_op jit(solution)/shard_map/ppermute | solution.py:13
  159.9 2.1 %fusion.2 = f32[128,128]{1,0:T(8,128)S(1)} fusion(pred[16,2]{1,0:T(8,128)(4,1)S(1)} %get-tuple-element.14, pred[16,2]{1,0:T(8,128)(4,1)S(1)} %get-tuple-element.13, pred[16,2]{1,0:T(8,128)(4,1)S(1)} %get-tuple-element.12, pred[16,2]{1,0:T(8,128)(4,1)S(1)} %get-tuple-element.11, bf16[16,128,128]{2,1,0:T(8,128)(2,1)S(1)} %constant_dynamic-update-slice_fusion, ...), kind=kOutput, calls=%fused_computation.8 | convolution fusion | flops 136855552 | bytes 3276944 | tf_op jit(solution)/shard_map/jspq,jspr->qr/dot_general | solution.py:43
  (127 shorter events, 15.6 us)
Async XLA Ops:
  6.5 47.2 %all-gather.2.cloned.1.call-start = ((), (), s32[]{:S(2)}) async-start(), calls=%async_computation | async-start | bytes 2228224 | tf_op jit(solution)/shard_map/all_gather | solution.py:33
  55.4 52.2 %copy-start.2 = (bf16[1,2048,128]{2,1,0:T(8,128)(2,1)}, bf16[1,2048,128]{2,1,0:T(8,128)(2,1)S(1)}, u32[]{:S(2)}) copy-start(bf16[1,2048,128]{2,1,0:T(8,128)(2,1)S(1)} %get-tuple-element.7) | copy-start | bytes 1572868
  57.8 6.1 %collective-permute-start = (bf16[1,128,128]{1,2,0:T(8,128)(2,1)S(1)}, bf16[1,128,128]{1,2,0:T(8,128)(2,1)S(1)}, u32[]{:S(2)}, u32[]{:S(2)}) collective-permute-start(bf16[1,128,128]{1,2,0:T(8,128)(2,1)S(1)} %fusion.47), channel_id=1, source_target_pairs={{0,1},{1,2},{2,3},{3,4},{4,5},{5,6},{6,7},{7,8},{8,9},{9,10},{10,1... | collective-permute-start | bytes 98312 | tf_op jit(solution)/shard_map/ppermute | solution.py:13
  58.1 6.0 %collective-permute-start.1 = (bf16[1,128,128]{1,2,0:T(8,128)(2,1)S(1)}, bf16[1,128,128]{1,2,0:T(8,128)(2,1)S(1)}, u32[]{:S(2)}, u32[]{:S(2)}) collective-permute-start(bf16[1,128,128]{1,2,0:T(8,128)(2,1)S(1)} %fusion.47), channel_id=1, source_target_pairs={{0,15},{1,0},{2,1},{3,2},{4,3},{5,4},{6,5},{7,6},{8,7},{9,8},{10,9... | collective-permute-start | bytes 98312 | tf_op jit(solution)/shard_map/ppermute | solution.py:16
  64.0 6.1 %collective-permute-start.2 = (bf16[1,128,128]{1,2,0:T(8,128)(2,1)S(1)}, bf16[1,128,128]{1,2,0:T(8,128)(2,1)S(1)}, u32[]{:S(2)}, u32[]{:S(2)}) collective-permute-start(bf16[1,128,128]{1,2,0:T(8,128)(2,1)S(1)} %collective-permute-done), channel_id=1, source_target_pairs={{0,1},{1,2},{2,3},{3,4},{4,5},{5,6},{6,7},{7,8},{8,9},{9,10},{10,1... | collective-permute-start | bytes 98312 | tf_op jit(solution)/shard_map/ppermute | solution.py:13
  64.2 6.1 %collective-permute-start.3 = (bf16[1,128,128]{1,2,0:T(8,128)(2,1)S(1)}, bf16[1,128,128]{1,2,0:T(8,128)(2,1)S(1)}, u32[]{:S(2)}, u32[]{:S(2)}) collective-permute-start(bf16[1,128,128]{1,2,0:T(8,128)(2,1)S(1)} %collective-permute-done.1), channel_id=1, source_target_pairs={{0,15},{1,0},{2,1},{3,2},{4,3},{5,4},{6,5},{7,6},{8,7},{9,8},{10,9... | collective-permute-start | bytes 98312 | tf_op jit(solution)/shard_map/ppermute | solution.py:16
  70.2 6.1 %collective-permute-start.4 = (bf16[1,128,128]{1,2,0:T(8,128)(2,1)S(1)}, bf16[1,128,128]{1,2,0:T(8,128)(2,1)S(1)}, u32[]{:S(2)}, u32[]{:S(2)}) collective-permute-start(bf16[1,128,128]{1,2,0:T(8,128)(2,1)S(1)} %collective-permute-done.2), channel_id=1, source_target_pairs={{0,1},{1,2},{2,3},{3,4},{4,5},{5,6},{6,7},{7,8},{8,9},{9,10},{10,1... | collective-permute-start | bytes 98312 | tf_op jit(solution)/shard_map/ppermute | solution.py:13
  70.4 6.1 %collective-permute-start.5 = (bf16[1,128,128]{1,2,0:T(8,128)(2,1)S(1)}, bf16[1,128,128]{1,2,0:T(8,128)(2,1)S(1)}, u32[]{:S(2)}, u32[]{:S(2)}) collective-permute-start(bf16[1,128,128]{1,2,0:T(8,128)(2,1)S(1)} %collective-permute-done.3), channel_id=1, source_target_pairs={{0,15},{1,0},{2,1},{3,2},{4,3},{5,4},{6,5},{7,6},{8,7},{9,8},{10,9... | collective-permute-start | bytes 98312 | tf_op jit(solution)/shard_map/ppermute | solution.py:16
  76.5 6.1 %collective-permute-start.6 = (bf16[1,128,128]{1,2,0:T(8,128)(2,1)S(1)}, bf16[1,128,128]{1,2,0:T(8,128)(2,1)S(1)}, u32[]{:S(2)}, u32[]{:S(2)}) collective-permute-start(bf16[1,128,128]{1,2,0:T(8,128)(2,1)S(1)} %collective-permute-done.4), channel_id=1, source_target_pairs={{0,1},{1,2},{2,3},{3,4},{4,5},{5,6},{6,7},{7,8},{8,9},{9,10},{10,1... | collective-permute-start | bytes 98312 | tf_op jit(solution)/shard_map/ppermute | solution.py:13
  76.7 6.1 %collective-permute-start.7 = (bf16[1,128,128]{1,2,0:T(8,128)(2,1)S(1)}, bf16[1,128,128]{1,2,0:T(8,128)(2,1)S(1)}, u32[]{:S(2)}, u32[]{:S(2)}) collective-permute-start(bf16[1,128,128]{1,2,0:T(8,128)(2,1)S(1)} %collective-permute-done.5), channel_id=1, source_target_pairs={{0,15},{1,0},{2,1},{3,2},{4,3},{5,4},{6,5},{7,6},{8,7},{9,8},{10,9... | collective-permute-start | bytes 98312 | tf_op jit(solution)/shard_map/ppermute | solution.py:16
  82.7 6.1 %collective-permute-start.8 = (bf16[1,128,128]{1,2,0:T(8,128)(2,1)S(1)}, bf16[1,128,128]{1,2,0:T(8,128)(2,1)S(1)}, u32[]{:S(2)}, u32[]{:S(2)}) collective-permute-start(bf16[1,128,128]{1,2,0:T(8,128)(2,1)S(1)} %collective-permute-done.6), channel_id=1, source_target_pairs={{0,1},{1,2},{2,3},{3,4},{4,5},{5,6},{6,7},{7,8},{8,9},{9,10},{10,1... | collective-permute-start | bytes 98312 | tf_op jit(solution)/shard_map/ppermute | solution.py:13
  82.9 6.1 %collective-permute-start.9 = (bf16[1,128,128]{1,2,0:T(8,128)(2,1)S(1)}, bf16[1,128,128]{1,2,0:T(8,128)(2,1)S(1)}, u32[]{:S(2)}, u32[]{:S(2)}) collective-permute-start(bf16[1,128,128]{1,2,0:T(8,128)(2,1)S(1)} %collective-permute-done.7), channel_id=1, source_target_pairs={{0,15},{1,0},{2,1},{3,2},{4,3},{5,4},{6,5},{7,6},{8,7},{9,8},{10,9... | collective-permute-start | bytes 98312 | tf_op jit(solution)/shard_map/ppermute | solution.py:16
  88.9 6.1 %collective-permute-start.10 = (bf16[1,128,128]{1,2,0:T(8,128)(2,1)S(1)}, bf16[1,128,128]{1,2,0:T(8,128)(2,1)S(1)}, u32[]{:S(2)}, u32[]{:S(2)}) collective-permute-start(bf16[1,128,128]{1,2,0:T(8,128)(2,1)S(1)} %collective-permute-done.8), channel_id=1, source_target_pairs={{0,1},{1,2},{2,3},{3,4},{4,5},{5,6},{6,7},{7,8},{8,9},{9,10},{10,1... | collective-permute-start | bytes 98312 | tf_op jit(solution)/shard_map/ppermute | solution.py:13
  89.1 6.1 %collective-permute-start.11 = (bf16[1,128,128]{1,2,0:T(8,128)(2,1)S(1)}, bf16[1,128,128]{1,2,0:T(8,128)(2,1)S(1)}, u32[]{:S(2)}, u32[]{:S(2)}) collective-permute-start(bf16[1,128,128]{1,2,0:T(8,128)(2,1)S(1)} %collective-permute-done.9), channel_id=1, source_target_pairs={{0,15},{1,0},{2,1},{3,2},{4,3},{5,4},{6,5},{7,6},{8,7},{9,8},{10,9... | collective-permute-start | bytes 98312 | tf_op jit(solution)/shard_map/ppermute | solution.py:16
  95.1 6.1 %collective-permute-start.12 = (bf16[1,128,128]{1,2,0:T(8,128)(2,1)S(1)}, bf16[1,128,128]{1,2,0:T(8,128)(2,1)S(1)}, u32[]{:S(2)}, u32[]{:S(2)}) collective-permute-start(bf16[1,128,128]{1,2,0:T(8,128)(2,1)S(1)} %collective-permute-done.10), channel_id=1, source_target_pairs={{0,1},{1,2},{2,3},{3,4},{4,5},{5,6},{6,7},{7,8},{8,9},{9,10},{10,1... | collective-permute-start | bytes 98312 | tf_op jit(solution)/shard_map/ppermute | solution.py:13
  95.3 6.1 %collective-permute-start.13 = (bf16[1,128,128]{1,2,0:T(8,128)(2,1)S(1)}, bf16[1,128,128]{1,2,0:T(8,128)(2,1)S(1)}, u32[]{:S(2)}, u32[]{:S(2)}) collective-permute-start(bf16[1,128,128]{1,2,0:T(8,128)(2,1)S(1)} %collective-permute-done.11), channel_id=1, source_target_pairs={{0,15},{1,0},{2,1},{3,2},{4,3},{5,4},{6,5},{7,6},{8,7},{9,8},{10,9... | collective-permute-start | bytes 98312 | tf_op jit(solution)/shard_map/ppermute | solution.py:16
  101.4 6.1 %collective-permute-start.14 = (bf16[1,128,128]{1,2,0:T(8,128)(2,1)S(1)}, bf16[1,128,128]{1,2,0:T(8,128)(2,1)S(1)}, u32[]{:S(2)}, u32[]{:S(2)}) collective-permute-start(bf16[1,128,128]{1,2,0:T(8,128)(2,1)S(1)} %collective-permute-done.12), channel_id=1, source_target_pairs={{0,1},{1,2},{2,3},{3,4},{4,5},{5,6},{6,7},{7,8},{8,9},{9,10},{10,1... | collective-permute-start | bytes 98312 | tf_op jit(solution)/shard_map/ppermute | solution.py:13
  110.1 6.1 %collective-permute-start.15 = (bf16[1,128,128]{1,2,0:T(8,128)(2,1)S(1)}, bf16[1,128,128]{1,2,0:T(8,128)(2,1)S(1)}, u32[]{:S(2)}, u32[]{:S(2)}) collective-permute-start(bf16[1,128,128]{1,2,0:T(8,128)(2,1)S(1)} %fusion.48), channel_id=1, source_target_pairs={{0,1},{1,2},{2,3},{3,4},{4,5},{5,6},{6,7},{7,8},{8,9},{9,10},{10,1... | collective-permute-start | bytes 98312 | tf_op jit(solution)/shard_map/ppermute | solution.py:13
  110.2 6.2 %collective-permute-start.16 = (bf16[1,128,128]{1,2,0:T(8,128)(2,1)S(1)}, bf16[1,128,128]{1,2,0:T(8,128)(2,1)S(1)}, u32[]{:S(2)}, u32[]{:S(2)}) collective-permute-start(bf16[1,128,128]{1,2,0:T(8,128)(2,1)S(1)} %fusion.48), channel_id=1, source_target_pairs={{0,15},{1,0},{2,1},{3,2},{4,3},{5,4},{6,5},{7,6},{8,7},{9,8},{10,9... | collective-permute-start | bytes 98312 | tf_op jit(solution)/shard_map/ppermute | solution.py:16
  116.4 6.1 %collective-permute-start.17 = (bf16[1,128,128]{1,2,0:T(8,128)(2,1)S(1)}, bf16[1,128,128]{1,2,0:T(8,128)(2,1)S(1)}, u32[]{:S(2)}, u32[]{:S(2)}) collective-permute-start(bf16[1,128,128]{1,2,0:T(8,128)(2,1)S(1)} %collective-permute-done.15), channel_id=1, source_target_pairs={{0,1},{1,2},{2,3},{3,4},{4,5},{5,6},{6,7},{7,8},{8,9},{9,10},{10,1... | collective-permute-start | bytes 98312 | tf_op jit(solution)/shard_map/ppermute | solution.py:13
  116.6 6.1 %collective-permute-start.18 = (bf16[1,128,128]{1,2,0:T(8,128)(2,1)S(1)}, bf16[1,128,128]{1,2,0:T(8,128)(2,1)S(1)}, u32[]{:S(2)}, u32[]{:S(2)}) collective-permute-start(bf16[1,128,128]{1,2,0:T(8,128)(2,1)S(1)} %collective-permute-done.16), channel_id=1, source_target_pairs={{0,15},{1,0},{2,1},{3,2},{4,3},{5,4},{6,5},{7,6},{8,7},{9,8},{10,9... | collective-permute-start | bytes 98312 | tf_op jit(solution)/shard_map/ppermute | solution.py:16
  122.6 6.1 %collective-permute-start.19 = (bf16[1,128,128]{1,2,0:T(8,128)(2,1)S(1)}, bf16[1,128,128]{1,2,0:T(8,128)(2,1)S(1)}, u32[]{:S(2)}, u32[]{:S(2)}) collective-permute-start(bf16[1,128,128]{1,2,0:T(8,128)(2,1)S(1)} %collective-permute-done.17), channel_id=1, source_target_pairs={{0,1},{1,2},{2,3},{3,4},{4,5},{5,6},{6,7},{7,8},{8,9},{9,10},{10,1... | collective-permute-start | bytes 98312 | tf_op jit(solution)/shard_map/ppermute | solution.py:13
  122.8 6.1 %collective-permute-start.20 = (bf16[1,128,128]{1,2,0:T(8,128)(2,1)S(1)}, bf16[1,128,128]{1,2,0:T(8,128)(2,1)S(1)}, u32[]{:S(2)}, u32[]{:S(2)}) collective-permute-start(bf16[1,128,128]{1,2,0:T(8,128)(2,1)S(1)} %collective-permute-done.18), channel_id=1, source_target_pairs={{0,15},{1,0},{2,1},{3,2},{4,3},{5,4},{6,5},{7,6},{8,7},{9,8},{10,9... | collective-permute-start | bytes 98312 | tf_op jit(solution)/shard_map/ppermute | solution.py:16
  128.8 6.1 %collective-permute-start.21 = (bf16[1,128,128]{1,2,0:T(8,128)(2,1)S(1)}, bf16[1,128,128]{1,2,0:T(8,128)(2,1)S(1)}, u32[]{:S(2)}, u32[]{:S(2)}) collective-permute-start(bf16[1,128,128]{1,2,0:T(8,128)(2,1)S(1)} %collective-permute-done.19), channel_id=1, source_target_pairs={{0,1},{1,2},{2,3},{3,4},{4,5},{5,6},{6,7},{7,8},{8,9},{9,10},{10,1... | collective-permute-start | bytes 98312 | tf_op jit(solution)/shard_map/ppermute | solution.py:13
  129.0 6.1 %collective-permute-start.22 = (bf16[1,128,128]{1,2,0:T(8,128)(2,1)S(1)}, bf16[1,128,128]{1,2,0:T(8,128)(2,1)S(1)}, u32[]{:S(2)}, u32[]{:S(2)}) collective-permute-start(bf16[1,128,128]{1,2,0:T(8,128)(2,1)S(1)} %collective-permute-done.20), channel_id=1, source_target_pairs={{0,15},{1,0},{2,1},{3,2},{4,3},{5,4},{6,5},{7,6},{8,7},{9,8},{10,9... | collective-permute-start | bytes 98312 | tf_op jit(solution)/shard_map/ppermute | solution.py:16
  135.0 6.1 %collective-permute-start.23 = (bf16[1,128,128]{1,2,0:T(8,128)(2,1)S(1)}, bf16[1,128,128]{1,2,0:T(8,128)(2,1)S(1)}, u32[]{:S(2)}, u32[]{:S(2)}) collective-permute-start(bf16[1,128,128]{1,2,0:T(8,128)(2,1)S(1)} %collective-permute-done.21), channel_id=1, source_target_pairs={{0,1},{1,2},{2,3},{3,4},{4,5},{5,6},{6,7},{7,8},{8,9},{9,10},{10,1... | collective-permute-start | bytes 98312 | tf_op jit(solution)/shard_map/ppermute | solution.py:13
  135.2 6.1 %collective-permute-start.24 = (bf16[1,128,128]{1,2,0:T(8,128)(2,1)S(1)}, bf16[1,128,128]{1,2,0:T(8,128)(2,1)S(1)}, u32[]{:S(2)}, u32[]{:S(2)}) collective-permute-start(bf16[1,128,128]{1,2,0:T(8,128)(2,1)S(1)} %collective-permute-done.22), channel_id=1, source_target_pairs={{0,15},{1,0},{2,1},{3,2},{4,3},{5,4},{6,5},{7,6},{8,7},{9,8},{10,9... | collective-permute-start | bytes 98312 | tf_op jit(solution)/shard_map/ppermute | solution.py:16
  141.3 6.1 %collective-permute-start.25 = (bf16[1,128,128]{1,2,0:T(8,128)(2,1)S(1)}, bf16[1,128,128]{1,2,0:T(8,128)(2,1)S(1)}, u32[]{:S(2)}, u32[]{:S(2)}) collective-permute-start(bf16[1,128,128]{1,2,0:T(8,128)(2,1)S(1)} %collective-permute-done.23), channel_id=1, source_target_pairs={{0,1},{1,2},{2,3},{3,4},{4,5},{5,6},{6,7},{7,8},{8,9},{9,10},{10,1... | collective-permute-start | bytes 98312 | tf_op jit(solution)/shard_map/ppermute | solution.py:13
  141.5 6.1 %collective-permute-start.26 = (bf16[1,128,128]{1,2,0:T(8,128)(2,1)S(1)}, bf16[1,128,128]{1,2,0:T(8,128)(2,1)S(1)}, u32[]{:S(2)}, u32[]{:S(2)}) collective-permute-start(bf16[1,128,128]{1,2,0:T(8,128)(2,1)S(1)} %collective-permute-done.24), channel_id=1, source_target_pairs={{0,15},{1,0},{2,1},{3,2},{4,3},{5,4},{6,5},{7,6},{8,7},{9,8},{10,9... | collective-permute-start | bytes 98312 | tf_op jit(solution)/shard_map/ppermute | solution.py:16
  147.5 6.1 %collective-permute-start.27 = (bf16[1,128,128]{1,2,0:T(8,128)(2,1)S(1)}, bf16[1,128,128]{1,2,0:T(8,128)(2,1)S(1)}, u32[]{:S(2)}, u32[]{:S(2)}) collective-permute-start(bf16[1,128,128]{1,2,0:T(8,128)(2,1)S(1)} %collective-permute-done.25), channel_id=1, source_target_pairs={{0,1},{1,2},{2,3},{3,4},{4,5},{5,6},{6,7},{7,8},{8,9},{9,10},{10,1... | collective-permute-start | bytes 98312 | tf_op jit(solution)/shard_map/ppermute | solution.py:13
  147.7 6.1 %collective-permute-start.28 = (bf16[1,128,128]{1,2,0:T(8,128)(2,1)S(1)}, bf16[1,128,128]{1,2,0:T(8,128)(2,1)S(1)}, u32[]{:S(2)}, u32[]{:S(2)}) collective-permute-start(bf16[1,128,128]{1,2,0:T(8,128)(2,1)S(1)} %collective-permute-done.26), channel_id=1, source_target_pairs={{0,15},{1,0},{2,1},{3,2},{4,3},{5,4},{6,5},{7,6},{8,7},{9,8},{10,9... | collective-permute-start | bytes 98312 | tf_op jit(solution)/shard_map/ppermute | solution.py:16
  153.7 6.1 %collective-permute-start.29 = (bf16[1,128,128]{1,2,0:T(8,128)(2,1)S(1)}, bf16[1,128,128]{1,2,0:T(8,128)(2,1)S(1)}, u32[]{:S(2)}, u32[]{:S(2)}) collective-permute-start(bf16[1,128,128]{1,2,0:T(8,128)(2,1)S(1)} %collective-permute-done.27), channel_id=1, source_target_pairs={{0,1},{1,2},{2,3},{3,4},{4,5},{5,6},{6,7},{7,8},{8,9},{9,10},{10,1... | collective-permute-start | bytes 98312 | tf_op jit(solution)/shard_map/ppermute | solution.py:13
  (4 other events, 10.1 us)
Sparse Core Ops, SparseCore 0:
  9.5 44.1 all-gather.1
